TPU v7x, 32 devices: a whole 2x2x4 slice. The times are simulated.
32 devices in a mesh: grp: 1, tok: 32 (over z, y, x, core).
Axes of the slice: x: 2, y: 2, z: 4, core: 2. Of those that a mesh axis runs over, the one named last changes fastest.
Arguments:
- activations: bfloat16 [65536, 2048], P('tok')
- out_grads: bfloat16 [65536, 512], P('tok')
- v_bank: bfloat16 [2048, 65536], P('tok'), may hold values from -0.125 to 0.125
- u_bank: bfloat16 [512, 65536], P('tok'), may hold values from -0.25 to 0.25
- query_ids: int32 [16], P('grp'), may hold values from 0 to 2047, as said below
Outputs:
- influence: float32 [65536, 16], P('tok', 'grp')
Inputs may be any that keep to these rules, and one draw needn't show every extreme that they name: `query_ids`: the ids are distinct; both 0 and 2047 are among them.
All inputs are finite; a program needn't handle non-finite values.
Results may differ from a plain program's by a relative error of at most 0.0003.
Values may be sent and summed in bfloat16 or wider, within the bound.
No kernel may reach another device: no remote copies, remote signals or barrier semaphores. Data moves between devices by JAX's collectives and lax.ppermute only.
A program may use at most 128 MiB of HBM per device.

v0:
```python
import jax
import jax.numpy as jnp
from jax import lax
from jax.sharding import PartitionSpec as P

RANK = 32


def select_columns(bank, query_ids):
    pieces = [
        lax.dynamic_slice_in_dim(bank, query_ids[q] * RANK, RANK, axis=1)
        for q in range(query_ids.shape[0])
    ]
    return jnp.concatenate(pieces, axis=1)


def folder(left, piece):
    return jnp.dot(left, piece, preferred_element_type=jnp.float32)


def total_over(x, axis):
    n = lax.axis_size(axis)
    copies = jnp.broadcast_to(x[None], (n,) + x.shape)
    return lax.all_to_all(copies, axis, 0, 0, tiled=False).sum(axis=0)


def on_device(activations, out_grads, v_bank, u_bank, query_ids):
    tok_rows = activations.shape[0]
    queries = query_ids.shape[0]
    v_sel = select_columns(v_bank, query_ids)
    u_sel = select_columns(u_bank, query_ids)
    proj_in = folder(activations, lax.all_gather(v_sel, "tok", axis=0, tiled=True))
    proj_out = folder(out_grads, lax.all_gather(u_sel, "tok", axis=0, tiled=True))
    scores = (proj_in * proj_out).reshape(tok_rows, queries, RANK).sum(axis=2)
    total = total_over(jnp.sum(scores * scores, axis=0), "tok")
    count = tok_rows * lax.axis_size("tok")
    scale = jnp.sqrt(total / count + 1e-06)
    return scores / scale[None, :]


def solution(mesh):
    return jax.shard_map(
        on_device,
        mesh=mesh,
        in_specs=(P("tok", None), P("tok", None), P("tok", None), P("tok", None), P("grp")),
        out_specs=P("tok", "grp"),
        check_vma=False,
    )
```

profile of v0, /device:TPU:0, one launch (start us, length us, event | category | flops | bytes accessed | tf_op | source)
XLA Modules:
  0.0 108.0 jit_solution(6873853208284179090)
XLA Ops:
  6.5 0.0 copy-start
  6.5 0.0 all-gather.2.cloned.1.call-start
  6.5 2.0 %fusion = (s32[1]{0:T(128)}, s32[1]{0:T(128)}, s32[1]{0:T(128)}, s32[1]{0:T(128)}, s32[1]{0:T(128)}, /*index=5*/s32[1]{0:T(128)}, s32[1]{0:T(128)}, s32[1]{0:T(1...) fusion(s32[16]{0:T(128)} %param.9), kind=kLoop, calls=%fused_computation.37 | loop fusion | bytes 128 | tf_op jit(solution)/shard_map/slice | solution.py:11
  18.6 1.1 %constant_dynamic-slice_fusion.16 = (bf16[64,32]{1,0:T(8,128)(2,1)S(1)}, bf16[64,32]{1,0:T(8,128)(2,1)S(1)}, bf16[64,32]{1,0:T(8,128)(2,1)S(1)}, bf16[64,32]{1,0...) fusion(bf16[64,65536]{1,0:T(8,128)(2,1)} %param.7, ...), kind=kLoop, calls=%fused_computation.20 | loop fusion | bytes 131136 | tf_op jit(solution)/shard_map/dynamic_slice | solution.py:11
  19.7 0.8 concatenate.6
  20.5 0.0 all-gather.2.cloned.1.call-update
  20.5 1.0 constant_dynamic-slice_fusion
  21.5 0.1 concatenate.7
  21.7 45.0 %all_gather.7 = bf16[512,512]{1,0:T(8,128)(2,1)S(1)} all-gather(bf16[16,512]{1,0:T(8,128)(2,1)S(1)} %concatenate.7), channel_id=1, replica_groups=mesh['grp'=1,'tok'=32] {'tok'}, dimensions={0}, use_global_device_ids=true | all-gather | bytes 540672 | tf_op jit(solution)/shard_map/all_gather | solution.py:33
  66.6 0.0 copy-done
  66.7 3.2 %fusion.1 = f32[512,2048]{1,0:T(8,128)} fusion(bf16[512,512]{1,0:T(8,128)(2,1)S(1)} %all_gather.7, bf16[2048,512]{1,0:T(8,128)(2,1)S(1)} %copy-done), kind=kOutput, calls=%fused_computation.38 | convolution fusion | flops 1073741824 | bytes 6815744 | tf_op jit(solution)/shard_map/dot_general | solution.py:18
  69.9 10.1 %all-gather.2.cloned.1.call-done = bf16[2048,512]{1,0:T(8,128)(2,1)} async-done(((bf16[64,512]{1,0:T(8,128)(2,1)}), bf16[2048,512]{1,0:T(8,128)(2,1)}) %all-gather.2.cloned.1.call-update) | async-done | bytes 2097168 | tf_op jit(solution)/shard_map/all_gather | solution.py:32
  80.0 9.8 %bitcast_reduce_fusion = f32[2048,16]{0,1:T(8,128)S(1)} fusion(f32[512,2048]{1,0:T(8,128)} %fusion.1, bf16[2048,512]{1,0:T(8,128)(2,1)} %all-gather.2.cloned.1.call-done, bf16[2048,2048]{1,0:T(8,128)(2,1)} %param.5), kind=kOutput, calls=%fused_computation | convolution fusion | flops 4297031680 | bytes 14811136 | tf_op jit(solution)/shard_map/dot_general | solution.py:18
  89.8 0.1 multiply_reduce_fusion
  89.9 10.4 %all_to_all.6 = f32[32,1,16]{2,1,0:T(1,128)S(1)} all-to-all(f32[32,1,16]{2,1,0:T(1,128)S(1)} %broadcast_in_dim.2), channel_id=1, replica_groups=mesh['grp'=1,'tok'=32] {'tok'}, dimensions={0} | all-to-all | bytes 4096 | tf_op jit(solution)/shard_map/all_to_all | solution.py:24
  100.3 0.1 reduce_sum.29
  100.4 0.7 broadcast_divide_fusion
  (2 shorter events, 0.0 us)
Async XLA Ops:
  6.5 60.1 %copy-start = (bf16[2048,512]{1,0:T(8,128)(2,1)S(1)}, bf16[2048,512]{1,0:T(8,128)(2,1)}, u32[]{:S(2)}) copy-start(bf16[2048,512]{1,0:T(8,128)(2,1)} %param.6) | copy-start | bytes 6291460
  6.5 73.5 %all-gather.2.cloned.1.call-start = ((), (), s32[]{:S(2)}) async-start(), calls=%async_computation.1 | async-start | bytes 2162688 | tf_op jit(solution)/shard_map/all_gather | solution.py:32
Sparse Core Ops, SparseCore 0:
  20.6 59.3 all-gather.1
where the time goes:
time: 108 us
  blocking collectives  55.4 us (51%)
  between operations  23.5 us (22%)
  matrix products  13 us (12%)
  waiting for transfers between devices  10.1 us (9%)
  local copies, waits for them, and re-layouts  4.99 us (5%)
    all_gather x1, blocking collectives, on_device(): lax.all_gather(u_sel, 'tok', axis=0, tiled=True)  45 us
    dot_general x2, matrix products, folder(): return jnp.dot(left, piece, preferred_element_type=jnp.float32)  13 us
    all_to_all x1, blocking collectives, total_over(): return lax.all_to_all(copies, axis, 0, 0, tiled=False).sum(axis=0)  10.4 us
    all_gather x1, waiting for transfers between devices, on_device(): lax.all_gather(v_sel, 'tok', axis=0, tiled=True)  10.1 us
  transfers between devices with their start and end apart: 1, of which 1 were waited for; matrix products, arithmetic and copies ran while one was open for 4% of the time, Pallas kernels for 0%

commit v1 on v0

--- a/solution.py
+++ b/solution.py
@@ -4,6 +4,34 @@
 from jax.sharding import PartitionSpec as P
 
 RANK = 32
+
+
+def expand_copies_over_axis(slab_in, join_dim):
+    taken_in = list(slab_in.shape[1:])
+    taken_in[join_dim] *= slab_in.shape[0]
+    return jnp.moveaxis(slab_in, 0, join_dim).reshape(taken_in)
+
+
+def report_run_for(z_in, chip_axis):
+    r2 = lax.axis_size(chip_axis)
+    y2 = lax.axis_index(chip_axis)
+    d_next, seen_now = (r2, y2)
+    local_part, earlier = (z_in[None], 1)
+    while earlier < d_next:
+        fresh = lax.ppermute(
+            local_part, axis_name=chip_axis, perm=[(ii, ii ^ earlier) for ii in range(d_next)]
+        )
+        a_next = seen_now & earlier == 0
+        local_part = jnp.concatenate(
+            [jnp.where(a_next, local_part, fresh), jnp.where(a_next, fresh, local_part)]
+        )
+        earlier *= 2
+    return local_part
+
+
+def answer_the_shapes(d0, local_array, x_local):
+    x_new = report_run_for(x_local, local_array)
+    return expand_copies_over_axis(x_new, d0)
 
 
 def select_columns(bank, query_ids):
@@ -29,7 +57,7 @@
     queries = query_ids.shape[0]
     v_sel = select_columns(v_bank, query_ids)
     u_sel = select_columns(u_bank, query_ids)
-    proj_in = folder(activations, lax.all_gather(v_sel, "tok", axis=0, tiled=True))
+    proj_in = folder(activations, answer_the_shapes(0, "tok", v_sel))
     proj_out = folder(out_grads, lax.all_gather(u_sel, "tok", axis=0, tiled=True))
     scores = (proj_in * proj_out).reshape(tok_rows, queries, RANK).sum(axis=2)
     total = total_over(jnp.sum(scores * scores, axis=0), "tok")

time: 108 us -> 142 us (1.31)
  blocking collectives: 55.4 us -> 80.7 us
  between operations: 23.5 us -> 10.3 us
  waiting for transfers between devices: 10.1 us -> 22 us
  starting transfers between devices: 0.01 us -> 9.01 us
  other arithmetic: 0.94 us -> 4.9 us
  matrix products: 13 us -> 9.83 us
    all_gather x1, blocking collectives: 45 us -> 69.4 us  [on_device(): lax.all_gather(u_sel, 'tok', axis=0, tiled=True)]
    ppermute x0 -> x5, waiting for transfers between devices: none -> 22 us  [report_run_for(): lax.ppermute(local_part, axis_name=chip_axis, perm=[(ii, ii ^ earlier) fo...]
    all_gather x1 -> x0, waiting for transfers between devices: 10.1 us -> none  [on_device(): lax.all_gather(v_sel, 'tok', axis=0, tiled=True)]
    ppermute x0 -> x5, starting transfers between devices: none -> 9.01 us  [report_run_for(): lax.ppermute(local_part, axis_name=chip_axis, perm=[(ii, ii ^ earlier) fo...]
    dot_general x2, matrix products: 13 us -> 9.83 us  [folder(): return jnp.dot(left, piece, preferred_element_type=jnp.float32)]
    select_n x0 -> x5, other arithmetic: none -> 2.63 us  [report_run_for(): jnp.where(a_next, local_part, fresh)]
  transfers between devices with their start and end apart: 1 -> 5, of which waited for: 1 -> 4; matrix products, arithmetic and copies ran while one was open for 4% -> 2% of each run, Pallas kernels for 0% -> 0%
where the time goes in v1:
time: 142 us
  blocking collectives  80.7 us (57%)
  waiting for transfers between devices  22 us (15%)
  between operations  10.3 us (7%)
  matrix products  9.83 us (7%)
  starting transfers between devices  9.01 us (6%)
  local copies, waits for them, and re-layouts  4.97 us (4%)
  other arithmetic  4.9 us (3%)
    all_gather x1, blocking collectives, on_device(): lax.all_gather(u_sel, 'tok', axis=0, tiled=True)  69.4 us
    ppermute x5, waiting for transfers between devices, report_run_for(): lax.ppermute(local_part, axis_name=chip_axis, perm=[(ii, ii ^ earlier) fo...  22 us
    all_to_all x1, blocking collectives, total_over(): return lax.all_to_all(copies, axis, 0, 0, tiled=False).sum(axis=0)  11.2 us
    dot_general x2, matrix products, folder(): return jnp.dot(left, piece, preferred_element_type=jnp.float32)  9.83 us
    ppermute x5, starting transfers between devices, report_run_for(): lax.ppermute(local_part, axis_name=chip_axis, perm=[(ii, ii ^ earlier) fo...  9.01 us
  transfers between devices with their start and end apart: 5, of which 4 were waited for; matrix products, arithmetic and copies ran while one was open for 2% of the time, Pallas kernels for 0%

profile of v1, /device:TPU:0, one launch (start us, length us, event | category | flops | bytes accessed | tf_op | source)
XLA Modules:
  0.0 141.6 jit_solution(13341683843244450950)
XLA Ops:
  0.0 0.0 copy-start
  0.0 2.0 %fusion = (s32[1]{0:T(128)}, s32[1]{0:T(128)}, s32[1]{0:T(128)}, s32[1]{0:T(128)}, s32[1]{0:T(128)}, /*index=5*/s32[1]{0:T(128)}, s32[1]{0:T(128)}, s32[1]{0:T(1...) fusion(s32[16]{0:T(128)} %param.9), kind=kLoop, calls=%fused_computation.52 | loop fusion | bytes 128 | tf_op jit(solution)/shard_map/slice | solution.py:39
  12.1 1.1 constant_dynamic-slice_fusion.16
  13.2 0.1 concatenate.21
  13.4 0.5 collective-permute-start
  13.9 0.9 collective-permute-done
  14.9 2.9 %collective-permute-start.1 = (bf16[2,64,512]{2,1,0:T(8,128)(2,1)S(1)}, bf16[2,64,512]{2,1,0:T(8,128)(2,1)S(1)}, u32[]{:S(2)}, u32[]{:S(2)}) collective-permute-start(bf16[2,64,512]{2,1,0:T(8,128)(2,1)S(1)} %pad_maximum_fusion.4), channel_id=1, source_target_pairs={{0,2},{1,3},{2,0},{3,1},{4,6},{5,7},{6,4},{7,5},{8,10},{9,11},{10,... | collective-permute-start | bytes 393224 | tf_op jit(solution)/shard_map/ppermute | solution.py:21
  17.8 3.8 %collective-permute-done.1 = bf16[2,64,512]{2,1,0:T(8,128)(2,1)S(1)} collective-permute-done((bf16[2,64,512]{2,1,0:T(8,128)(2,1)S(1)}, bf16[2,64,512]{2,1,0:T(8,128)(2,1)S(1)}, u32[]{:S(2)}, u32[]{:S(2)}) %collective-permute-start.1) | collective-permute-done | bytes 131104 | tf_op jit(solution)/shard_map/ppermute | solution.py:21
  21.6 1.8 %collective-permute-start.2 = (bf16[4,64,512]{2,1,0:T(8,128)(2,1)S(1)}, bf16[4,64,512]{2,1,0:T(8,128)(2,1)S(1)}, u32[]{:S(2)}, u32[]{:S(2)}) collective-permute-start(bf16[4,64,512]{2,1,0:T(8,128)(2,1)S(1)} %pad_maximum_fusion.3), channel_id=1, source_target_pairs={{0,4},{1,5},{2,6},{3,7},{4,0},{5,1},{6,2},{7,3},{8,12},{9,13},{10,... | collective-permute-start | bytes 786440 | tf_op jit(solution)/shard_map/ppermute | solution.py:21
  23.5 6.1 %collective-permute-done.2 = bf16[4,64,512]{2,1,0:T(8,128)(2,1)S(1)} collective-permute-done((bf16[4,64,512]{2,1,0:T(8,128)(2,1)S(1)}, bf16[4,64,512]{2,1,0:T(8,128)(2,1)S(1)}, u32[]{:S(2)}, u32[]{:S(2)}) %collective-permute-start.2) | collective-permute-done | bytes 262176 | tf_op jit(solution)/shard_map/ppermute | solution.py:21
  29.6 0.0 copy-start.1
  29.6 0.7 copy-done.1
  30.4 1.6 %collective-permute-start.3 = (bf16[8,64,512]{2,1,0:T(8,128)(2,1)S(1)}, bf16[8,64,512]{2,1,0:T(8,128)(2,1)}, u32[]{:S(2)}, u32[]{:S(2)}) collective-permute-start(bf16[8,64,512]{2,1,0:T(8,128)(2,1)S(1)} %pad_maximum_fusion.2), channel_id=1, source_target_pairs={{0,8},{1,9},{2,10},{3,11},{4,12},{5,13},{6,14},{7,15},{8,0},{9,1},... | collective-permute-start | bytes 1572872 | tf_op jit(solution)/shard_map/ppermute | solution.py:21
  31.9 11.2 %collective-permute-done.3 = bf16[8,64,512]{2,1,0:T(8,128)(2,1)} collective-permute-done((bf16[8,64,512]{2,1,0:T(8,128)(2,1)S(1)}, bf16[8,64,512]{2,1,0:T(8,128)(2,1)}, u32[]{:S(2)}, u32[]{:S(2)}) %collective-permute-start.3) | collective-permute-done | bytes 524320 | tf_op jit(solution)/shard_map/ppermute | solution.py:21
  43.1 1.2 broadcast_select_fusion.3
  44.3 1.1 pad_maximum_fusion.1
  45.3 2.2 %collective-permute-start.4 = (bf16[16,64,512]{2,1,0:T(8,128)(2,1)}, bf16[16,64,512]{2,1,0:T(8,128)(2,1)}, u32[]{:S(2)}, u32[]{:S(2)}) collective-permute-start(bf16[16,64,512]{2,1,0:T(8,128)(2,1)} %pad_maximum_fusion.1), channel_id=1, source_target_pairs={{0,16},{1,17},{2,18},{3,19},{4,20},{5,21},{6,22},{7,23},{8,24},{9,... | collective-permute-start | bytes 3145736 | tf_op jit(solution)/shard_map/ppermute | solution.py:21
  47.5 0.9 constant_dynamic-slice_fusion
  48.5 0.1 concatenate.27
  48.6 69.4 %all_gather.3 = bf16[512,512]{1,0:T(8,128)(2,1)S(1)} all-gather(bf16[16,512]{1,0:T(8,128)(2,1)S(1)} %concatenate.27), channel_id=1, replica_groups=mesh['grp'=1,'tok'=32] {'tok'}, dimensions={0}, use_global_device_ids=true | all-gather | bytes 540672 | tf_op jit(solution)/shard_map/all_gather | solution.py:61
  118.0 0.0 copy-done
  118.0 1.3 fusion.1
  119.3 0.0 collective-permute-done.4
  119.3 1.4 broadcast_select_fusion.1
  120.7 0.2 pad_maximum_fusion
  120.9 8.5 %bitcast_reduce_fusion = f32[2048,16]{0,1:T(8,128)S(1)} fusion(f32[512,2048]{1,0:T(8,128)S(1)} %fusion.1, bf16[2048,512]{1,0:T(8,128)(2,1)S(1)} %bitcast.28, bf16[2048,2048]{1,0:T(8,128)(2,1)} %param.5), kind=kOutput, calls=%fused_computation | convolution fusion | flops 4297031680 | bytes 14811136 | tf_op jit(solution)/shard_map/dot_general | solution.py:46
  129.4 0.1 multiply_reduce_fusion
  129.6 11.2 %all_to_all.6 = f32[32,1,16]{2,1,0:T(1,128)S(1)} all-to-all(f32[32,1,16]{2,1,0:T(1,128)S(1)} %broadcast_in_dim.5), channel_id=1, replica_groups=mesh['grp'=1,'tok'=32] {'tok'}, dimensions={0} | all-to-all | bytes 4096 | tf_op jit(solution)/shard_map/all_to_all | solution.py:52
  140.8 0.1 reduce_sum.29
  140.9 0.7 broadcast_divide_fusion
  (8 shorter events, 0.2 us)
Async XLA Ops:
  0.0 118.0 %copy-start = (bf16[2048,512]{1,0:T(8,128)(2,1)S(1)}, bf16[2048,512]{1,0:T(8,128)(2,1)}, u32[]{:S(2)}) copy-start(bf16[2048,512]{1,0:T(8,128)(2,1)} %param.6) | copy-start | bytes 6291460
  13.4 1.4 %collective-permute-start = (bf16[1,64,512]{2,1,0:T(8,128)(2,1)S(1)}, bf16[1,64,512]{2,1,0:T(8,128)(2,1)S(1)}, u32[]{:S(2)}, u32[]{:S(2)}) collective-permute-start(bf16[1,64,512]{2,1,0:T(8,128)(2,1)S(1)} %bitcast.29), channel_id=1, source_target_pairs={{0,1},{1,0},{2,3},{3,2},{4,5},{5,4},{6,7},{7,6},{8,9},{9,8},{10,11... | collective-permute-start | bytes 196616 | tf_op jit(solution)/shard_map/ppermute | solution.py:21
  14.9 6.7 %collective-permute-start.1 = (bf16[2,64,512]{2,1,0:T(8,128)(2,1)S(1)}, bf16[2,64,512]{2,1,0:T(8,128)(2,1)S(1)}, u32[]{:S(2)}, u32[]{:S(2)}) collective-permute-start(bf16[2,64,512]{2,1,0:T(8,128)(2,1)S(1)} %pad_maximum_fusion.4), channel_id=1, source_target_pairs={{0,2},{1,3},{2,0},{3,1},{4,6},{5,7},{6,4},{7,5},{8,10},{9,11},{10,... | collective-permute-start | bytes 393224 | tf_op jit(solution)/shard_map/ppermute | solution.py:21
  21.6 7.9 %collective-permute-start.2 = (bf16[4,64,512]{2,1,0:T(8,128)(2,1)S(1)}, bf16[4,64,512]{2,1,0:T(8,128)(2,1)S(1)}, u32[]{:S(2)}, u32[]{:S(2)}) collective-permute-start(bf16[4,64,512]{2,1,0:T(8,128)(2,1)S(1)} %pad_maximum_fusion.3), channel_id=1, source_target_pairs={{0,4},{1,5},{2,6},{3,7},{4,0},{5,1},{6,2},{7,3},{8,12},{9,13},{10,... | collective-permute-start | bytes 786440 | tf_op jit(solution)/shard_map/ppermute | solution.py:21
  29.6 0.7 copy-start.1
  30.4 12.7 %collective-permute-start.3 = (bf16[8,64,512]{2,1,0:T(8,128)(2,1)S(1)}, bf16[8,64,512]{2,1,0:T(8,128)(2,1)}, u32[]{:S(2)}, u32[]{:S(2)}) collective-permute-start(bf16[8,64,512]{2,1,0:T(8,128)(2,1)S(1)} %pad_maximum_fusion.2), channel_id=1, source_target_pairs={{0,8},{1,9},{2,10},{3,11},{4,12},{5,13},{6,14},{7,15},{8,0},{9,1},... | collective-permute-start | bytes 1572872 | tf_op jit(solution)/shard_map/ppermute | solution.py:21
  45.3 74.0 %collective-permute-start.4 = (bf16[16,64,512]{2,1,0:T(8,128)(2,1)}, bf16[16,64,512]{2,1,0:T(8,128)(2,1)}, u32[]{:S(2)}, u32[]{:S(2)}) collective-permute-start(bf16[16,64,512]{2,1,0:T(8,128)(2,1)} %pad_maximum_fusion.1), channel_id=1, source_target_pairs={{0,16},{1,17},{2,18},{3,19},{4,20},{5,21},{6,22},{7,23},{8,24},{9,... | collective-permute-start | bytes 3145736 | tf_op jit(solution)/shard_map/ppermute | solution.py:21
